TPU v7x, 128 devices: a whole 4x4x4 slice. The times are simulated.
128 devices in a mesh: grp: 4 (over z), dev: 32 (over x, y, core).
Axes of the slice: x: 4, y: 4, z: 4, core: 2. Of those that a mesh axis runs over, the one named last changes fastest.
Arguments:
- packed_w: bfloat16 [4, 8192, 8192], P(None, 'dev', 'grp'), may hold values from -0.0625 to 0.0625
- packed_t: bfloat16 [4, 8192, 1536], P(None, 'dev', 'grp'), may hold values from -6 to 6
- row_energy: float32 [4, 8192], P('grp', 'dev'), may hold values from 0.3 to 4
- col_energy: float32 [4, 1536], P('grp'), may hold values from 0.3 to 4
- block_order: int32 [4], replicated, may hold values from 3072 to 8192, as said below
Outputs:
- new_amps: float32 [4, 8192, 1536], P(None, 'dev', 'grp')
Inputs may be any that keep to these rules, and one draw needn't show every extreme that they name: `block_order`: one block has order exactly 8192; the others lie between 3072 and 8191.
All inputs are finite; a program needn't handle non-finite values.
Results may differ from a plain program's by a relative error of at most 0.0003.
Values may be sent and summed in bfloat16 or wider, within the bound.
No kernel may reach another device: no remote copies, remote signals or barrier semaphores. Data moves between devices by JAX's collectives and lax.ppermute only.
A program may use at most 192 MiB of HBM per device.

v0:
```python
import jax
import jax.numpy as jnp
from jax import lax
from jax.sharding import Mesh, NamedSharding, PartitionSpec as P


def apply_update(t_rows, cycle, live, row_gap, col_gap):
    denom = row_gap[:, None] + col_gap[None, :]
    update = jnp.where(live[:, None], cycle / denom, jnp.zeros_like(cycle))
    return t_rows.astype(jnp.float32) + update


def shards(packed_w, packed_t, row_energy, col_energy, block_order):
    nchip = lax.axis_size("chip")
    ncore = lax.axis_size("dc")
    rank = lax.axis_index("chip") * ncore + lax.axis_index("dc")
    group = lax.axis_index("grp")
    local = packed_t.shape[1]
    ndev = nchip * ncore
    true_rows = jnp.arange(local, dtype=jnp.int32) * ndev + rank
    t_rows = lax.all_to_all(packed_t, "grp", split_axis=0, concat_axis=2, tiled=True)[0]
    order = lax.dynamic_index_in_dim(block_order, group, 0, keepdims=False)
    live = true_rows < order
    t_live = jnp.where(live[:, None], t_rows, jnp.zeros_like(t_rows))
    t_half = lax.all_gather(t_live, "chip", axis=0, tiled=True)
    w_rows = lax.all_to_all(packed_w, "grp", split_axis=0, concat_axis=2, tiled=True)[0]
    w4 = w_rows.reshape(local, nchip, ncore, local)
    w_mine = lax.all_to_all(w4, "dc", split_axis=2, concat_axis=0, tiled=True)
    w_mine = w_mine.reshape(ncore * local, nchip * local)
    partial = jnp.dot(w_mine, t_half, preferred_element_type=jnp.float32)
    cycle = lax.psum_scatter(partial, "dc", scatter_dimension=0, tiled=True)
    new_block = apply_update(t_rows, cycle, live, row_energy[0], col_energy[0])
    return lax.all_to_all(new_block[None], "grp", split_axis=2, concat_axis=0, tiled=True)


def solution(mesh):
    ngrp, ndev = mesh.devices.shape
    ncore = 2
    split = Mesh(mesh.devices.reshape(ngrp, ndev // ncore, ncore), ("grp", "chip", "dc"))
    rows = ("chip", "dc")
    in_specs = (P(None, rows, "grp"), P(None, rows, "grp"), P("grp", rows), P("grp", None), P())
    out_specs = P(None, rows, "grp")
    body = jax.shard_map(
        shards, mesh=split, in_specs=in_specs, out_specs=out_specs, check_vma=False
    )
    target = NamedSharding(mesh, P(None, "dev", "grp"))

    def run(*args):
        return lax.with_sharding_constraint(body(*args), target)

    return run
```

profile of v0, /device:TPU:0, one launch (start us, length us, event | category | flops | bytes accessed | tf_op | source)
XLA Modules:
  0.0 192.1 jit_solution(3250268429148516764)
XLA Ops:
  6.5 5.4 %all-to-all-start = ((bf16[4,256,384]{2,1,0:T(8,128)(2,1)}), bf16[4,256,384]{2,1,0:T(8,128)(2,1)S(1)}, u32[]{:S(2)}, u32[]{:S(2)}) async-start(bf16[4,256,384]{2,1,0:T(8,128)(2,1)} %param.6), calls=%async_computation | async-start | bytes 1572864 | tf_op jit(solution)/shard_map/all_to_all | solution.py:21
  12.0 0.0 all-gather.2.cloned.1.call-start
  12.0 1.2 dynamic_slice.4
  13.2 0.7 add_compare_fusion
  13.8 10.4 %all-to-all-done = bf16[4,256,384]{2,1,0:T(8,128)(2,1)S(1)} async-done(((bf16[4,256,384]{2,1,0:T(8,128)(2,1)}), bf16[4,256,384]{2,1,0:T(8,128)(2,1)S(1)}, u32[]{:S(2)}, u32[]{:S(2)}) %all-to-all-start) | async-done | bytes 786464 | tf_op jit(solution)/shard_map/all_to_all | solution.py:21
  24.2 0.3 copy.12
  24.5 1.0 bitcast_select_fusion
  25.5 0.0 all-gather.2.cloned.1.call-update
  25.5 0.0 reduce-scatter.2.cloned.1.call-start
  25.6 6.2 %copy.13 = bf16[4,256,2048]{1,2,0:T(8,128)(2,1)} copy(bf16[4,256,2048]{2,1,0:T(8,128)(2,1)} %param.5) | data formatting | bytes 8388608 | tf_op args[0]
  31.8 51.7 %all_to_all.63 = bf16[4,256,2048]{1,2,0:T(8,128)(2,1)S(1)} all-to-all(bf16[4,256,2048]{1,2,0:T(8,128)(2,1)} %copy.13), channel_id=1, replica_groups=mesh['grp'=4,'chip'=16,'dc'=2] {'grp'}, dimensions={0} | all-to-all | bytes 8388608 | tf_op jit(solution)/shard_map/all_to_all | solution.py:26
  83.5 0.4 copy.14
  83.9 8.2 %all_to_all.64 = bf16[256,16,2,256]{0,3,1,2:T(8,128)(2,1)} all-to-all(bf16[256,16,2,256]{0,3,1,2:T(8,128)(2,1)S(1)} %copy.14), channel_id=1, replica_groups=mesh['grp'=4,'chip'=16,'dc'=2] {'dc'}, dimensions={2} | all-to-all | bytes 8388608 | tf_op jit(solution)/shard_map/all_to_all | solution.py:28
  92.1 7.9 %copy.15 = bf16[2,256,16,1,256]{4,2,1,0,3:T(8,128)(2,1)} copy(bf16[2,256,16,1,256]{1,4,2,0,3:T(8,128)(2,1)} %bitcast.31) | data formatting | bytes 8388608 | tf_op jit(solution)/shard_map/all_to_all | solution.py:28
  100.0 6.3 %copy.18 = bf16[64,8,16,256]{3,1,2,0:T(8,128)(2,1)} copy(bf16[64,8,16,256]{3,2,1,0:T(8,128)(2,1)} %bitcast.32) | data formatting | bytes 8388608
  106.4 17.2 %all-gather.2.cloned.1.call-done = bf16[4096,1536]{0,1:T(8,128)(2,1)} async-done(((bf16[256,1536]{0,1:T(8,128)(2,1)}), bf16[4096,1536]{0,1:T(8,128)(2,1)}) %all-gather.2.cloned.1.call-update) | async-done | bytes 12582928 | tf_op jit(solution)/shard_map/all_gather | solution.py:25
  123.5 12.1 %convolution_bitcast_fusion = f32[512,1536]{0,1:T(8,128)} fusion(bf16[4096,1536]{0,1:T(8,128)(2,1)} %all-gather.2.cloned.1.call-done, bf16[512,4096]{1,0:T(8,128)(2,1)} %bitcast.34), kind=kOutput, calls=%fused_computation | convolution fusion | flops 6442450944 | bytes 19922944 | tf_op jit(solution)/shard_map/dot_general | solution.py:30
  135.6 0.0 copy-start
  135.6 0.0 copy-start.1
  135.6 0.0 reduce-scatter.2.cloned.1.call-update
  135.6 0.7 copy-done
  136.3 12.6 %reduce-scatter.2.cloned.1.call-done = f32[256,1536]{0,1:T(8,128)} async-done(((f32[512,1536]{0,1:T(8,128)}), f32[256,1536]{0,1:T(8,128)}) %reduce-scatter.2.cloned.1.call-update) | async-done | bytes 1572880 | tf_op jit(solution)/shard_map/reduce_scatter | solution.py:31
  148.9 0.0 copy-done.1
  148.9 1.8 add_bitcast_fusion
  150.7 6.5 %copy.16 = f32[1,256,1536]{1,0,2:T(1,128)S(1)} copy(f32[1,256,1536]{1,2,0:T(8,128)S(1)} %add_bitcast_fusion) | data formatting | bytes 3145728 | tf_op jit(solution)/shard_map/broadcast_in_dim | solution.py:33
  157.2 25.3 %all_to_all.65 = f32[1,256,1536]{1,0,2:T(1,128)S(1)} all-to-all(f32[1,256,1536]{1,0,2:T(1,128)S(1)} %copy.16), channel_id=1, replica_groups=mesh['grp'=4,'chip'=16,'dc'=2] {'grp'}, dimensions={2} | all-to-all | bytes 3145728 | tf_op jit(solution)/shard_map/all_to_all | solution.py:33
  182.5 2.7 %copy.17 = f32[1,256,4,384]{3,1,2,0:T(8,128)} copy(f32[1,256,4,384]{1,0,3,2:T(1,128)S(1)} %bitcast.33) | data formatting | bytes 3145728 | tf_op jit(solution)/shard_map/all_to_all | solution.py:33
  (1 shorter events, 0.0 us)
Async XLA Ops:
  6.5 17.7 %all-to-all-start = ((bf16[4,256,384]{2,1,0:T(8,128)(2,1)}), bf16[4,256,384]{2,1,0:T(8,128)(2,1)S(1)}, u32[]{:S(2)}, u32[]{:S(2)}) async-start(bf16[4,256,384]{2,1,0:T(8,128)(2,1)} %param.6), calls=%async_computation | async-start | bytes 1572864 | tf_op jit(solution)/shard_map/all_to_all | solution.py:21
  12.0 111.6 %all-gather.2.cloned.1.call-start = ((), (), s32[]{:S(2)}) async-start(), calls=%async_computation.5 | async-start | bytes 13369344 | tf_op jit(solution)/shard_map/all_gather | solution.py:25
  25.5 123.4 %reduce-scatter.2.cloned.1.call-start = ((), (), s32[]{:S(2)}) async-start(), calls=%async_computation.6 | async-start | bytes 4718592 | tf_op jit(solution)/shard_map/reduce_scatter | solution.py:31
  135.6 0.7 copy-start
  135.6 13.3 %copy-start.1 = (f32[1,256]{1,0:T(1,128)S(1)}, f32[1,256]{1,0:T(1,128)}, u32[]{:S(2)}) copy-start(f32[1,256]{1,0:T(1,128)} %param.7) | copy-start | bytes 3076
Sparse Core Ops, SparseCore 0:
  25.7 97.8 all-gather.1
  135.7 13.1 reduce-scatter.1
where the time goes:
time: 193 us; the launch traced here: 192 us
  blocking collectives  85.2 us (44%)
  waiting for transfers between devices  40.2 us (21%)
  local copies, waits for them, and re-layouts  32.3 us (17%)
  between operations  13.4 us (7%)
  matrix products  12.1 us (6%)
  starting transfers between devices  5.46 us (3%)
  other arithmetic  3.45 us (2%)
    all_to_all x1, blocking collectives, shards(): lax.all_to_all(packed_w, 'grp', split_axis=0, concat_axis=2, tiled=True)[0]  51.7 us
    all_to_all x1, blocking collectives, shards(): lax.all_to_all(new_block[None], 'grp', split_axis=2, concat_axis=0, tiled...  25.3 us
    all_gather x1, waiting for transfers between devices, shards(): t_half = lax.all_gather(t_live, 'chip', axis=0, tiled=True)  17.2 us
    unnamed x6, local copies, waits for them, and re-layouts  13.2 us
    reduce_scatter x1, waiting for transfers between devices, shards(): cycle = lax.psum_scatter(partial, 'dc', scatter_dimension=0, tiled=True)  12.6 us
    dot_general x1, matrix products, shards(): partial = jnp.dot(w_mine, t_half, preferred_element_type=jnp.float32)  12.1 us
    all_to_all x1, waiting for transfers between devices, shards(): lax.all_to_all(packed_t, 'grp', split_axis=0, concat_axis=2, tiled=True)[0]  10.4 us
    all_to_all x1, blocking collectives, shards(): w_mine = lax.all_to_all(w4, 'dc', split_axis=2, concat_axis=0, tiled=True)  8.16 us
  transfers between devices with their start and end apart: 3, of which 3 were waited for; matrix products, arithmetic and copies ran while one was open for 12% of the time, Pallas kernels for 0%

commit v1 on v0

--- a/solution.py
+++ b/solution.py
@@ -22,7 +22,9 @@
     order = lax.dynamic_index_in_dim(block_order, group, 0, keepdims=False)
     live = true_rows < order
     t_live = jnp.where(live[:, None], t_rows, jnp.zeros_like(t_rows))
-    t_half = lax.all_gather(t_live, "chip", axis=0, tiled=True)
+    t_half = jnp.concatenate(
+        lax.all_to_all(jnp.stack([t_live] * lax.axis_size("chip")), "chip", 0, 0), axis=0
+    )
     w_rows = lax.all_to_all(packed_w, "grp", split_axis=0, concat_axis=2, tiled=True)[0]
     w4 = w_rows.reshape(local, nchip, ncore, local)
     w_mine = lax.all_to_all(w4, "dc", split_axis=2, concat_axis=0, tiled=True)

time: 193 us -> 391 us (2.03)
  waiting for transfers between devices: 40.2 us -> 272 us
  blocking collectives: 85.2 us -> 33.5 us
  starting transfers between devices: 5.46 us -> 17.4 us
  local copies, waits for them, and re-layouts: 32.3 us -> 39.8 us
    all_to_all x0 -> x2, waiting for transfers between devices: none -> 248 us  [the longest x1 202 us: shards(): lax.all_to_all(jnp.stack([t_live] * lax.axis_size('chip')), 'chip', 0, 0)]
    all_to_all x1 -> x0, blocking collectives: 51.7 us -> none  [shards(): lax.all_to_all(packed_w, 'grp', split_axis=0, concat_axis=2, tiled=True)[0]]
    all_gather x1 -> x0, waiting for transfers between devices: 17.2 us -> none  [shards(): t_half = lax.all_gather(t_live, 'chip', axis=0, tiled=True)]
    all_to_all x0 -> x2, starting transfers between devices: none -> 11.9 us  [the longest x1 7.08 us: shards(): lax.all_to_all(jnp.stack([t_live] * lax.axis_size('chip')), 'chip', 0, 0)]
    another operation x0 -> x1, local copies, waits for them, and re-layouts: none -> 5.69 us  [shards(): jnp.stack([t_live] * lax.axis_size('chip'))]
    reduce_scatter x1, waiting for transfers between devices: 12.6 us -> 18 us  [shards(): cycle = lax.psum_scatter(partial, 'dc', scatter_dimension=0, tiled=True)]
    all_to_all x1, waiting for transfers between devices: 10.4 us -> 6.03 us  [shards(): lax.all_to_all(packed_t, 'grp', split_axis=0, concat_axis=2, tiled=True)[0]]
    unnamed x6 -> x8, local copies, waits for them, and re-layouts: 13.2 us -> 13.3 us
  transfers between devices with their start and end apart: 3 -> 4, of which waited for: 3 -> 4; matrix products, arithmetic and copies ran while one was open for 12% -> 6% of each run, Pallas kernels for 0% -> 0%
where the time goes in v1:
time: 391 us
  waiting for transfers between devices  272 us (70%)
  local copies, waits for them, and re-layouts  39.8 us (10%)
  blocking collectives  33.5 us (9%)
  starting transfers between devices  17.4 us (4%)
  between operations  13.5 us (3%)
  matrix products  12.1 us (3%)
    all_to_all x1, waiting for transfers between devices, shards(): lax.all_to_all(jnp.stack([t_live] * lax.axis_size('chip')), 'chip', 0, 0)  202 us
    all_to_all x1, waiting for transfers between devices, shards(): lax.all_to_all(packed_w, 'grp', split_axis=0, concat_axis=2, tiled=True)[0]  46.1 us
    all_to_all x1, blocking collectives, shards(): lax.all_to_all(new_block[None], 'grp', split_axis=2, concat_axis=0, tiled...  25.3 us
    reduce_scatter x1, waiting for transfers between devices, shards(): cycle = lax.psum_scatter(partial, 'dc', scatter_dimension=0, tiled=True)  18 us
    unnamed x8, local copies, waits for them, and re-layouts  13.3 us
    dot_general x1, matrix products, shards(): partial = jnp.dot(w_mine, t_half, preferred_element_type=jnp.float32)  12.1 us
    all_to_all x1, blocking collectives, shards(): w_mine = lax.all_to_all(w4, 'dc', split_axis=2, concat_axis=0, tiled=True)  8.18 us
    all_to_all x1, local copies, waits for them, and re-layouts, shards(): w_mine = lax.all_to_all(w4, 'dc', split_axis=2, concat_axis=0, tiled=True)  7.99 us
  transfers between devices with their start and end apart: 4, of which 4 were waited for; matrix products, arithmetic and copies ran while one was open for 6% of the time, Pallas kernels for 0%

profile of v1, /device:TPU:0, one launch (start us, length us, event | category | flops | bytes accessed | tf_op | source)
XLA Modules:
  0.0 390.6 jit_solution(894100575223617009)
XLA Ops:
  6.5 5.4 %all-to-all-start = ((bf16[4,256,384]{2,1,0:T(8,128)(2,1)}), bf16[4,256,384]{2,1,0:T(8,128)(2,1)S(1)}, u32[]{:S(2)}, u32[]{:S(2)}) async-start(bf16[4,256,384]{2,1,0:T(8,128)(2,1)} %param.6), calls=%async_computation | async-start | bytes 1572864 | tf_op jit(solution)/shard_map/all_to_all | solution.py:21
  12.0 6.3 %copy.16 = bf16[4,256,2048]{1,2,0:T(8,128)(2,1)} copy(bf16[4,256,2048]{2,1,0:T(8,128)(2,1)} %param.5) | data formatting | bytes 8388608 | tf_op args[0]
  18.2 0.0 copy-start.2
  18.2 6.0 %all-to-all-done = bf16[4,256,384]{2,1,0:T(8,128)(2,1)S(1)} async-done(((bf16[4,256,384]{2,1,0:T(8,128)(2,1)}), bf16[4,256,384]{2,1,0:T(8,128)(2,1)S(1)}, u32[]{:S(2)}, u32[]{:S(2)}) %all-to-all-start) | async-done | bytes 786464 | tf_op jit(solution)/shard_map/all_to_all | solution.py:21
  24.2 4.8 %all-to-all-start.2 = ((bf16[4,256,2048]{1,2,0:T(8,128)(2,1)}), bf16[4,256,2048]{1,2,0:T(8,128)(2,1)}, u32[]{:S(2)}, u32[]{:S(2)}) async-start(bf16[4,256,2048]{1,2,0:T(8,128)(2,1)} %copy.16), calls=%async_computation.2 | async-start | bytes 8388608 | tf_op jit(solution)/shard_map/all_to_all | solution.py:28
  29.1 0.0 copy-done.2
  29.1 0.6 dynamic_slice.4
  29.7 0.7 add_compare_fusion
  30.3 0.3 copy.14
  30.6 0.1 bitcast_select_fusion
  30.7 0.3 copy.15
  31.0 46.1 %all-to-all-done.2 = bf16[4,256,2048]{1,2,0:T(8,128)(2,1)} async-done(((bf16[4,256,2048]{1,2,0:T(8,128)(2,1)}), bf16[4,256,2048]{1,2,0:T(8,128)(2,1)}, u32[]{:S(2)}, u32[]{:S(2)}) %all-to-all-start.2) | async-done | bytes 4194336 | tf_op jit(solution)/shard_map/all_to_all | solution.py:28
  77.1 2.5 copy.17
  79.6 8.2 %all_to_all.68 = bf16[256,16,2,256]{0,3,1,2:T(8,128)(2,1)} all-to-all(bf16[256,16,2,256]{0,3,1,2:T(8,128)(2,1)S(1)} %copy.17), channel_id=1, replica_groups=mesh['grp'=4,'chip'=16,'dc'=2] {'dc'}, dimensions={2} | all-to-all | bytes 8388608 | tf_op jit(solution)/shard_map/all_to_all | solution.py:30
  87.7 5.7 %stack.2 = bf16[16,256,1536]{2,1,0:T(8,128)(2,1)} broadcast(bf16[256,1536]{1,0:T(8,128)(2,1)S(1)} %copy.15), dimensions={1,2} | broadcast | bytes 13369344 | tf_op jit(solution)/shard_map/stack | solution.py:26
  93.4 7.1 %all-to-all-start.1 = ((bf16[16,256,1536]{2,1,0:T(8,128)(2,1)}), bf16[16,256,1536]{2,1,0:T(8,128)(2,1)}, u32[]{:S(2)}, u32[]{:S(2)}) async-start(bf16[16,256,1536]{2,1,0:T(8,128)(2,1)} %stack.2), calls=%async_computation.1 | async-start | bytes 25165824 | tf_op jit(solution)/shard_map/all_to_all | solution.py:26
  100.5 0.0 reduce-scatter.2.cloned.1.call-start
  100.6 8.0 %copy.18 = bf16[2,256,16,1,256]{4,2,1,0,3:T(8,128)(2,1)} copy(bf16[2,256,16,1,256]{1,4,2,0,3:T(8,128)(2,1)} %bitcast.31) | data formatting | bytes 8388608 | tf_op jit(solution)/shard_map/all_to_all | solution.py:30
  108.5 6.4 %copy.21 = bf16[64,8,16,256]{3,1,2,0:T(8,128)(2,1)} copy(bf16[64,8,16,256]{3,2,1,0:T(8,128)(2,1)} %bitcast.32) | data formatting | bytes 8388608
  114.9 201.6 %all-to-all-done.1 = bf16[16,256,1536]{2,1,0:T(8,128)(2,1)} async-done(((bf16[16,256,1536]{2,1,0:T(8,128)(2,1)}), bf16[16,256,1536]{2,1,0:T(8,128)(2,1)}, u32[]{:S(2)}, u32[]{:S(2)}) %all-to-all-start.1) | async-done | bytes 12582944 | tf_op jit(solution)/shard_map/all_to_all | solution.py:26
  316.6 12.1 %convolution_bitcast_fusion = f32[512,1536]{0,1:T(8,128)} fusion(bf16[4096,1536]{1,0:T(8,128)(2,1)} %bitcast.4, bf16[512,4096]{1,0:T(8,128)(2,1)} %bitcast.34), kind=kOutput, calls=%fused_computation | convolution fusion | flops 6442450944 | bytes 19922944 | tf_op jit(solution)/shard_map/dot_general | solution.py:32
  328.6 0.0 copy-start
  328.6 0.0 copy-start.1
  328.7 0.0 reduce-scatter.2.cloned.1.call-update
  328.7 0.7 copy-done
  329.4 18.0 %reduce-scatter.2.cloned.1.call-done = f32[256,1536]{0,1:T(8,128)} async-done(((f32[512,1536]{0,1:T(8,128)}), f32[256,1536]{0,1:T(8,128)}) %reduce-scatter.2.cloned.1.call-update) | async-done | bytes 1572880 | tf_op jit(solution)/shard_map/reduce_scatter | solution.py:33
  347.4 0.0 copy-done.1
  347.4 1.8 add_bitcast_fusion
  349.2 6.5 %copy.19 = f32[1,256,1536]{1,0,2:T(1,128)S(1)} copy(f32[1,256,1536]{1,2,0:T(8,128)S(1)} %add_bitcast_fusion) | data formatting | bytes 3145728 | tf_op jit(solution)/shard_map/broadcast_in_dim | solution.py:35
  355.7 25.3 %all_to_all.69 = f32[1,256,1536]{1,0,2:T(1,128)S(1)} all-to-all(f32[1,256,1536]{1,0,2:T(1,128)S(1)} %copy.19), channel_id=1, replica_groups=mesh['grp'=4,'chip'=16,'dc'=2] {'grp'}, dimensions={2} | all-to-all | bytes 3145728 | tf_op jit(solution)/shard_map/all_to_all | solution.py:35
  381.0 2.7 copy.20
  (1 shorter events, 0.0 us)
Async XLA Ops:
  6.5 17.7 %all-to-all-start = ((bf16[4,256,384]{2,1,0:T(8,128)(2,1)}), bf16[4,256,384]{2,1,0:T(8,128)(2,1)S(1)}, u32[]{:S(2)}, u32[]{:S(2)}) async-start(bf16[4,256,384]{2,1,0:T(8,128)(2,1)} %param.6), calls=%async_computation | async-start | bytes 1572864 | tf_op jit(solution)/shard_map/all_to_all | solution.py:21
  18.2 10.9 %copy-start.2 = (s32[4]{0:T(128)S(1)}, s32[4]{0:T(128)}, u32[]{:S(2)}) copy-start(s32[4]{0:T(128)} %param.9) | copy-start | bytes 52
  24.2 52.9 %all-to-all-start.2 = ((bf16[4,256,2048]{1,2,0:T(8,128)(2,1)}), bf16[4,256,2048]{1,2,0:T(8,128)(2,1)}, u32[]{:S(2)}, u32[]{:S(2)}) async-start(bf16[4,256,2048]{1,2,0:T(8,128)(2,1)} %copy.16), calls=%async_computation.2 | async-start | bytes 8388608 | tf_op jit(solution)/shard_map/all_to_all | solution.py:28
  93.4 223.1 %all-to-all-start.1 = ((bf16[16,256,1536]{2,1,0:T(8,128)(2,1)}), bf16[16,256,1536]{2,1,0:T(8,128)(2,1)}, u32[]{:S(2)}, u32[]{:S(2)}) async-start(bf16[16,256,1536]{2,1,0:T(8,128)(2,1)} %stack.2), calls=%async_computation.1 | async-start | bytes 25165824 | tf_op jit(solution)/shard_map/all_to_all | solution.py:26
  100.5 246.9 %reduce-scatter.2.cloned.1.call-start = ((), (), s32[]{:S(2)}) async-start(), calls=%async_computation.6 | async-start | bytes 4718592 | tf_op jit(solution)/shard_map/reduce_scatter | solution.py:33
  328.6 0.7 copy-start
  328.6 18.8 %copy-start.1 = (f32[1,256]{1,0:T(1,128)S(1)}, f32[1,256]{1,0:T(1,128)}, u32[]{:S(2)}) copy-start(f32[1,256]{1,0:T(1,128)} %param.7) | copy-start | bytes 3076
Sparse Core Ops, SparseCore 0:
  328.8 18.5 reduce-scatter.1
